TPU v7x, 512 devices: a whole 4x8x8 slice. The times are simulated.
512 devices in a mesh: seq: 64 (over z_hi, y, core), tp: 8 (over x, z_lo).
Axes of the slice: x: 4, y: 8, z: 8 (z_hi: 4, z_lo: 2; z = z_hi * 2 + z_lo), core: 2. Of those that a mesh axis runs over, the one named last changes fastest.
Arguments:
- query_proj: bfloat16 [16384, 3072], P('seq', 'tp'), may hold values from -8 to 8
- key_proj: bfloat16 [16384, 3072], P('seq', 'tp'), may hold values from -8 to 8
- value_proj: bfloat16 [16384, 3072], P('seq', 'tp'), may hold values from -6 to 6
- hidden: bfloat16 [16384, 3072], P('seq', 'tp'), may hold values from -2 to 2
- out_weight: bfloat16 [3072, 3072], P('tp'), may hold values from -0.109375 to 0.109375
- norm_gain: bfloat16 [3072], P('tp'), may hold values from 0.099609375 to 1.8984375
- segment_ids: int32 [16384], P('seq'), may hold values from 0 to 31, never falling along the last dimension, each value on 1 to 8192 neighbouring positions
- pad_mask: int32 [16384], P('seq'), may hold values 0 or 1
- page_table: int32 [128], P('seq'), may hold values from 0 to 1, as said below
Outputs:
- hidden_out: bfloat16 [16384, 3072], P('seq', 'tp')
- normed: bfloat16 [16384, 3072], P('seq', 'tp')
- kv_pages: bfloat16 [128, 2, 128, 3072], P('seq', None, None, 'tp')
Inputs may be any that keep to these rules, and one draw needn't show every extreme that they name: `segment_ids`: never falling along the tokens; each of the 32 prompts has 1 to 8192 tokens, one exactly 8192. `page_table`: the 2 pages of each aligned block of 2 pages name each slot once.
All inputs are finite; a program needn't handle non-finite values. No bound on the sum of `pad_mask` on one device may be relied on, other than what follows from the above.
Results may differ from a plain program's by a relative error of at most 0.014.
Values may be sent and summed in bfloat16 or wider, within the bound.
No kernel may reach another device: no remote copies, remote signals or barrier semaphores. Data moves between devices by JAX's collectives and lax.ppermute only.
A program may use at most 128 MiB of HBM per device.

v0:
```python
import math
import jax
import jax.numpy as jnp
from jax import lax
from jax.sharding import PartitionSpec as P

D = 3072
HEAD_DIM = 96
PAGE = 128
far_index = 1073741824
masked_score = -1e30
norm_epsilon = 1e-05


def passed_along(block, axis, distance):
    devices = range(lax.axis_size(axis))
    route = [(i - distance, i) for i in devices if i - distance in devices]
    return lax.ppermute(block, axis, route)


def rotate(values_in, position, head_count, head_dim):
    count_rows = values_in.shape[0]
    half_dim = head_dim // 2
    frequency = jnp.exp(
        jnp.arange(half_dim, dtype=jnp.float32) * (-2.0 * math.log(10000.0) / head_dim)
    )
    angles = position.astype(jnp.float32)[:, None] * frequency[None, :]
    cosine = jnp.cos(angles)[:, None, :]
    sine_part = jnp.sin(angles)[:, None, :]
    as_float = values_in.astype(jnp.float32).reshape(count_rows, head_count, head_dim)
    lower_half = as_float[..., :half_dim]
    upper_half = as_float[..., half_dim:]
    rotated = jnp.concatenate(
        [
            lower_half * cosine - upper_half * sine_part,
            upper_half * cosine + lower_half * sine_part,
        ],
        axis=-1,
    )
    return rotated.reshape(count_rows, head_count * head_dim).astype(jnp.bfloat16)


def attend(softmax_state, query_heads, block, visible):
    row_peak, row_total, weighted = softmax_state
    key_count = block.shape[1]
    head_count = query_heads.shape[1]
    key_heads = block[0].reshape(key_count, head_count, HEAD_DIM)
    val_heads = block[1].reshape(key_count, head_count, HEAD_DIM)
    factor = 1.0 / math.sqrt(HEAD_DIM)
    logits = (
        jnp.einsum("qhd,khd->hqk", query_heads, key_heads, preferred_element_type=jnp.float32)
        * factor
    )
    logits = jnp.where(visible[None], logits, masked_score)
    new_peak = jnp.maximum(row_peak, jnp.max(logits, axis=-1))
    rescale = jnp.exp(row_peak - new_peak)
    unnormed = jnp.where(visible[None], jnp.exp(logits - new_peak[..., None]), 0.0)
    row_total = row_total * rescale + jnp.sum(unnormed, axis=-1)
    weighted = weighted * rescale[..., None] + jnp.einsum(
        "hqk,khd->hqd", unnormed.astype(jnp.bfloat16), val_heads, preferred_element_type=jnp.float32
    )
    return (new_peak, row_total, weighted)


def per_device(
    query_proj,
    key_proj,
    value_proj,
    hidden,
    out_weight,
    norm_gain,
    segment_ids,
    pad_mask,
    page_table,
):
    tok_count = query_proj.shape[0]
    feat_count = query_proj.shape[1]
    head_count = feat_count // HEAD_DIM
    seg_count = lax.axis_size("seq") // 2
    reach_count = lax.axis_size("seq") // 2
    device_row = lax.axis_index("seq")
    tok_index = device_row * tok_count + jnp.arange(tok_count, dtype=jnp.int32)
    member = segment_ids[:, None] == jnp.arange(seg_count, dtype=jnp.int32)[None, :]
    local_first = jnp.min(jnp.where(member, tok_index[:, None], far_index), axis=0)
    first_tok = lax.pmin(local_first, "seq")
    position = tok_index - jnp.sum(jnp.where(member, first_tok[None, :], 0), axis=1)
    q_rot = rotate(query_proj, position, head_count, HEAD_DIM)
    k_rot = rotate(key_proj, position, head_count, HEAD_DIM)
    query_heads = q_rot.reshape(tok_count, head_count, HEAD_DIM)
    query_tag = segment_ids + 1
    key_tag = jnp.where(pad_mask == 1, segment_ids + 1, 0)
    tag_rows = -(-tok_count // feat_count)
    tag_block = jnp.pad(key_tag.astype(jnp.bfloat16), (0, tag_rows * feat_count - tok_count))
    own_block = jnp.concatenate(
        [k_rot, value_proj, tag_block.reshape(tag_rows, feat_count)], axis=0
    )
    offsets = jnp.arange(tok_count, dtype=jnp.int32)
    own_visible = (key_tag[None, :] == query_tag[:, None]) & (
        offsets[None, :] <= offsets[:, None]
    ) | (offsets[None, :] == offsets[:, None])
    softmax_state = (
        jnp.full((head_count, tok_count), masked_score, jnp.float32),
        jnp.zeros((head_count, tok_count), jnp.float32),
        jnp.zeros((head_count, tok_count, HEAD_DIM), jnp.float32),
    )
    softmax_state = attend(softmax_state, query_heads, jnp.stack([k_rot, value_proj]), own_visible)
    query_tag_wide = query_tag.astype(jnp.bfloat16)

    def visit_block(current, moved):
        pair = moved[: 2 * tok_count].reshape(2, tok_count, feat_count)
        moved_tags = moved[2 * tok_count :].reshape(-1)[:tok_count]
        visible = moved_tags[None, :] == query_tag_wide[:, None]
        return attend(current, query_heads, pair, visible)

    def cycle_turn(turn_index, loop_state):
        current, moved = loop_state
        following = passed_along(moved, "seq", 1)
        return (visit_block(current, moved), following)

    moved = passed_along(own_block, "seq", 1)
    softmax_state, moved = lax.fori_loop(0, reach_count - 1, cycle_turn, (softmax_state, moved))
    softmax_state = visit_block(softmax_state, moved)
    row_peak, row_total, weighted = softmax_state
    attn = (
        jnp.transpose(weighted / row_total[..., None], (1, 0, 2))
        .reshape(tok_count, feat_count)
        .astype(jnp.bfloat16)
    )
    partial_value = jnp.dot(attn, out_weight, preferred_element_type=jnp.float32)
    feature_width = hidden.shape[1]
    own_sum = lax.psum_scatter(
        partial_value.astype(jnp.bfloat16), "tp", scatter_dimension=1, tiled=True
    ).astype(jnp.float32)
    hidden_out = (hidden.astype(jnp.float32) + own_sum).astype(jnp.bfloat16)
    stream_wide = hidden_out.astype(jnp.float32)
    square_total = lax.psum(jnp.sum(stream_wide * stream_wide, axis=1), "tp")
    normed = (
        stream_wide
        * lax.rsqrt(square_total / D + norm_epsilon)[:, None]
        * norm_gain.astype(jnp.float32)[None, :]
    ).astype(jnp.bfloat16)
    pad_scale = pad_mask.astype(jnp.bfloat16)[:, None]
    page_count = tok_count // PAGE
    stacked = jnp.stack([k_rot * pad_scale, value_proj * pad_scale])
    stacked = stacked.reshape(2, page_count, PAGE, feat_count).transpose(1, 0, 2, 3)
    kv_pages = jnp.zeros_like(stacked).at[page_table].set(stacked)
    return (hidden_out, normed, kv_pages)


def solution(mesh):
    placed = (
        P("seq", "tp"),
        P("seq", "tp"),
        P("seq", "tp"),
        P("seq", "tp"),
        P("tp", None),
        P("tp"),
        P("seq"),
        P("seq"),
        P("seq"),
    )
    return jax.shard_map(
        per_device,
        mesh=mesh,
        in_specs=placed,
        out_specs=(P("seq", "tp"), P("seq", "tp"), P("seq", None, None, "tp")),
        check_vma=False,
    )
```

profile of v0, /device:TPU:8, one launch (start us, length us, event | category | flops | bytes accessed | tf_op | source)
XLA Modules:
  0.0 678.9 jit_solution(2169950836960678962)
XLA Ops:
  8.2 28.3 %pmin.7 = s32[32]{0:T(128)S(1)} all-reduce(s32[32]{0:T(128)S(1)} %select_reduce_fusion.1), channel_id=1, replica_groups=mesh['seq'=64,'tp'=8] {'seq'}, use_global_device_ids=true, to_apply=%region_1.2 | all-reduce | flops 32 | bytes 256 | tf_op jit(solution)/shard_map/pmin | solution.py:85
  50.9 443.5 %while.16 = (s32[]{:T(128)}, f32[4,256]{1,0:T(4,128)S(1)}, f32[4,256]{1,0:T(4,128)S(1)}, f32[4,256,96]{1,2,0:T(8,128)}, bf16[513,384]{1,0:T(8,128)(2,1)}, /*inde...) while((s32[]{:T(128)}, f32[4,256]{1,0:T(4,128)S(1)}, f32[4,256]{1,0:T(4,128)S(1)}, ...), condition=%wide.region_8.9_spmd, body=%wide.region_5.8_spmd.sunk | while | flops 103286784 | bytes 8788605 | solution.py:121
  111.1 3.4 collective-permute-start
  160.9 3.3 collective-permute-start
  210.7 3.5 collective-permute-start
  223.4 9.2 %collective-permute-start = (bf16[513,384]{1,0:T(8,128)(2,1)}, bf16[513,384]{1,0:T(8,128)(2,1)}, u32[]{:S(2)}, u32[]{:S(2)}) collective-permute-start(bf16[513,384]{1,0:T(8,128)(2,1)} %copy.78), channel_id=1, source_target_pairs={{0,8},{8,16},{16,24},{24,32},{32,40},{40,48},{48,56},{56,64},{64,7... | collective-permute-start | bytes 1181960 | tf_op jit(solution)/shard_map/while/body/eval_jaxpr/ppermute | solution.py:18
  241.7 8.9 %collective-permute-start = (bf16[513,384]{1,0:T(8,128)(2,1)}, bf16[513,384]{1,0:T(8,128)(2,1)}, u32[]{:S(2)}, u32[]{:S(2)}) collective-permute-start(bf16[513,384]{1,0:T(8,128)(2,1)} %copy.78), channel_id=1, source_target_pairs={{0,8},{8,16},{16,24},{24,32},{32,40},{40,48},{48,56},{56,64},{64,7... | collective-permute-start | bytes 1181960 | tf_op jit(solution)/shard_map/while/body/eval_jaxpr/ppermute | solution.py:18
  259.8 9.4 %collective-permute-start = (bf16[513,384]{1,0:T(8,128)(2,1)}, bf16[513,384]{1,0:T(8,128)(2,1)}, u32[]{:S(2)}, u32[]{:S(2)}) collective-permute-start(bf16[513,384]{1,0:T(8,128)(2,1)} %copy.78), channel_id=1, source_target_pairs={{0,8},{8,16},{16,24},{24,32},{32,40},{40,48},{48,56},{56,64},{64,7... | collective-permute-start | bytes 1181960 | tf_op jit(solution)/shard_map/while/body/eval_jaxpr/ppermute | solution.py:18
  278.3 9.2 %collective-permute-start = (bf16[513,384]{1,0:T(8,128)(2,1)}, bf16[513,384]{1,0:T(8,128)(2,1)}, u32[]{:S(2)}, u32[]{:S(2)}) collective-permute-start(bf16[513,384]{1,0:T(8,128)(2,1)} %copy.78), channel_id=1, source_target_pairs={{0,8},{8,16},{16,24},{24,32},{32,40},{40,48},{48,56},{56,64},{64,7... | collective-permute-start | bytes 1181960 | tf_op jit(solution)/shard_map/while/body/eval_jaxpr/ppermute | solution.py:18
  296.6 8.4 %collective-permute-start = (bf16[513,384]{1,0:T(8,128)(2,1)}, bf16[513,384]{1,0:T(8,128)(2,1)}, u32[]{:S(2)}, u32[]{:S(2)}) collective-permute-start(bf16[513,384]{1,0:T(8,128)(2,1)} %copy.78), channel_id=1, source_target_pairs={{0,8},{8,16},{16,24},{24,32},{32,40},{40,48},{48,56},{56,64},{64,7... | collective-permute-start | bytes 1181960 | tf_op jit(solution)/shard_map/while/body/eval_jaxpr/ppermute | solution.py:18
  314.2 7.1 %collective-permute-start = (bf16[513,384]{1,0:T(8,128)(2,1)}, bf16[513,384]{1,0:T(8,128)(2,1)}, u32[]{:S(2)}, u32[]{:S(2)}) collective-permute-start(bf16[513,384]{1,0:T(8,128)(2,1)} %copy.78), channel_id=1, source_target_pairs={{0,8},{8,16},{16,24},{24,32},{32,40},{40,48},{48,56},{56,64},{64,7... | collective-permute-start | bytes 1181960 | tf_op jit(solution)/shard_map/while/body/eval_jaxpr/ppermute | solution.py:18
  330.4 5.1 collective-permute-start
  344.7 5.1 collective-permute-start
  358.9 5.1 collective-permute-start
  373.2 5.7 collective-permute-start
  388.1 6.5 collective-permute-start
  403.6 6.5 collective-permute-start
  419.3 6.4 collective-permute-start
  434.7 6.3 collective-permute-start
  450.2 6.2 collective-permute-start
  465.5 6.2 collective-permute-start
  480.8 6.2 collective-permute-start
  504.7 146.8 %reduce-scatter.4.cloned.1.call-done = bf16[384,256]{1,0:T(8,128)(2,1)} async-done(((bf16[3072,256]{1,0:T(8,128)(2,1)}), bf16[384,256]{1,0:T(8,128)(2,1)}) %reduce-scatter.4.cloned.1.call-update) | async-done | bytes 196624
  652.8 18.4 %psum.7 = f32[256]{0:T(256)S(1)} all-reduce(f32[256]{0:T(256)S(1)} %get-tuple-element.63), channel_id=1, replica_groups=mesh['seq'=64,'tp'=8] {'tp'}, use_global_device_ids=true, to_apply=%region_13.14 | all-reduce | flops 256 | bytes 2048 | tf_op jit(solution)/shard_map/psum | solution.py:136
  (497 shorter events, 341.9 us)
Async XLA Ops:
  7.2 644.4 %reduce-scatter.4.cloned.1.call-start = ((), (), s32[]{:S(2)}) async-start(), calls=%async_computation.1 | async-start | bytes 1769472
  111.1 10.7 %collective-permute-start = (bf16[513,384]{1,0:T(8,128)(2,1)}, bf16[513,384]{1,0:T(8,128)(2,1)}, u32[]{:S(2)}, u32[]{:S(2)}) collective-permute-start(bf16[513,384]{1,0:T(8,128)(2,1)} %copy.78), channel_id=1, source_target_pairs={{0,8},{8,16},{16,24},{24,32},{32,40},{40,48},{48,56},{56,64},{64,7... | collective-permute-start | bytes 1181960 | tf_op jit(solution)/shard_map/while/body/eval_jaxpr/ppermute | solution.py:18
  123.6 10.7 %collective-permute-start = (bf16[513,384]{1,0:T(8,128)(2,1)}, bf16[513,384]{1,0:T(8,128)(2,1)}, u32[]{:S(2)}, u32[]{:S(2)}) collective-permute-start(bf16[513,384]{1,0:T(8,128)(2,1)} %copy.78), channel_id=1, source_target_pairs={{0,8},{8,16},{16,24},{24,32},{32,40},{40,48},{48,56},{56,64},{64,7... | collective-permute-start | bytes 1181960 | tf_op jit(solution)/shard_map/while/body/eval_jaxpr/ppermute | solution.py:18
  160.9 10.7 %collective-permute-start = (bf16[513,384]{1,0:T(8,128)(2,1)}, bf16[513,384]{1,0:T(8,128)(2,1)}, u32[]{:S(2)}, u32[]{:S(2)}) collective-permute-start(bf16[513,384]{1,0:T(8,128)(2,1)} %copy.78), channel_id=1, source_target_pairs={{0,8},{8,16},{16,24},{24,32},{32,40},{40,48},{48,56},{56,64},{64,7... | collective-permute-start | bytes 1181960 | tf_op jit(solution)/shard_map/while/body/eval_jaxpr/ppermute | solution.py:18
  173.4 10.7 %collective-permute-start = (bf16[513,384]{1,0:T(8,128)(2,1)}, bf16[513,384]{1,0:T(8,128)(2,1)}, u32[]{:S(2)}, u32[]{:S(2)}) collective-permute-start(bf16[513,384]{1,0:T(8,128)(2,1)} %copy.78), channel_id=1, source_target_pairs={{0,8},{8,16},{16,24},{24,32},{32,40},{40,48},{48,56},{56,64},{64,7... | collective-permute-start | bytes 1181960 | tf_op jit(solution)/shard_map/while/body/eval_jaxpr/ppermute | solution.py:18
  198.3 10.7 %collective-permute-start = (bf16[513,384]{1,0:T(8,128)(2,1)}, bf16[513,384]{1,0:T(8,128)(2,1)}, u32[]{:S(2)}, u32[]{:S(2)}) collective-permute-start(bf16[513,384]{1,0:T(8,128)(2,1)} %copy.78), channel_id=1, source_target_pairs={{0,8},{8,16},{16,24},{24,32},{32,40},{40,48},{48,56},{56,64},{64,7... | collective-permute-start | bytes 1181960 | tf_op jit(solution)/shard_map/while/body/eval_jaxpr/ppermute | solution.py:18
  210.7 10.9 %collective-permute-start = (bf16[513,384]{1,0:T(8,128)(2,1)}, bf16[513,384]{1,0:T(8,128)(2,1)}, u32[]{:S(2)}, u32[]{:S(2)}) collective-permute-start(bf16[513,384]{1,0:T(8,128)(2,1)} %copy.78), channel_id=1, source_target_pairs={{0,8},{8,16},{16,24},{24,32},{32,40},{40,48},{48,56},{56,64},{64,7... | collective-permute-start | bytes 1181960 | tf_op jit(solution)/shard_map/while/body/eval_jaxpr/ppermute | solution.py:18
  223.4 16.5 %collective-permute-start = (bf16[513,384]{1,0:T(8,128)(2,1)}, bf16[513,384]{1,0:T(8,128)(2,1)}, u32[]{:S(2)}, u32[]{:S(2)}) collective-permute-start(bf16[513,384]{1,0:T(8,128)(2,1)} %copy.78), channel_id=1, source_target_pairs={{0,8},{8,16},{16,24},{24,32},{32,40},{40,48},{48,56},{56,64},{64,7... | collective-permute-start | bytes 1181960 | tf_op jit(solution)/shard_map/while/body/eval_jaxpr/ppermute | solution.py:18
  241.7 16.3 %collective-permute-start = (bf16[513,384]{1,0:T(8,128)(2,1)}, bf16[513,384]{1,0:T(8,128)(2,1)}, u32[]{:S(2)}, u32[]{:S(2)}) collective-permute-start(bf16[513,384]{1,0:T(8,128)(2,1)} %copy.78), channel_id=1, source_target_pairs={{0,8},{8,16},{16,24},{24,32},{32,40},{40,48},{48,56},{56,64},{64,7... | collective-permute-start | bytes 1181960 | tf_op jit(solution)/shard_map/while/body/eval_jaxpr/ppermute | solution.py:18
  259.8 16.8 %collective-permute-start = (bf16[513,384]{1,0:T(8,128)(2,1)}, bf16[513,384]{1,0:T(8,128)(2,1)}, u32[]{:S(2)}, u32[]{:S(2)}) collective-permute-start(bf16[513,384]{1,0:T(8,128)(2,1)} %copy.78), channel_id=1, source_target_pairs={{0,8},{8,16},{16,24},{24,32},{32,40},{40,48},{48,56},{56,64},{64,7... | collective-permute-start | bytes 1181960 | tf_op jit(solution)/shard_map/while/body/eval_jaxpr/ppermute | solution.py:18
  278.3 16.6 %collective-permute-start = (bf16[513,384]{1,0:T(8,128)(2,1)}, bf16[513,384]{1,0:T(8,128)(2,1)}, u32[]{:S(2)}, u32[]{:S(2)}) collective-permute-start(bf16[513,384]{1,0:T(8,128)(2,1)} %copy.78), channel_id=1, source_target_pairs={{0,8},{8,16},{16,24},{24,32},{32,40},{40,48},{48,56},{56,64},{64,7... | collective-permute-start | bytes 1181960 | tf_op jit(solution)/shard_map/while/body/eval_jaxpr/ppermute | solution.py:18
  296.6 15.8 %collective-permute-start = (bf16[513,384]{1,0:T(8,128)(2,1)}, bf16[513,384]{1,0:T(8,128)(2,1)}, u32[]{:S(2)}, u32[]{:S(2)}) collective-permute-start(bf16[513,384]{1,0:T(8,128)(2,1)} %copy.78), channel_id=1, source_target_pairs={{0,8},{8,16},{16,24},{24,32},{32,40},{40,48},{48,56},{56,64},{64,7... | collective-permute-start | bytes 1181960 | tf_op jit(solution)/shard_map/while/body/eval_jaxpr/ppermute | solution.py:18
  314.2 14.5 %collective-permute-start = (bf16[513,384]{1,0:T(8,128)(2,1)}, bf16[513,384]{1,0:T(8,128)(2,1)}, u32[]{:S(2)}, u32[]{:S(2)}) collective-permute-start(bf16[513,384]{1,0:T(8,128)(2,1)} %copy.78), channel_id=1, source_target_pairs={{0,8},{8,16},{16,24},{24,32},{32,40},{40,48},{48,56},{56,64},{64,7... | collective-permute-start | bytes 1181960 | tf_op jit(solution)/shard_map/while/body/eval_jaxpr/ppermute | solution.py:18
  330.4 12.5 %collective-permute-start = (bf16[513,384]{1,0:T(8,128)(2,1)}, bf16[513,384]{1,0:T(8,128)(2,1)}, u32[]{:S(2)}, u32[]{:S(2)}) collective-permute-start(bf16[513,384]{1,0:T(8,128)(2,1)} %copy.78), channel_id=1, source_target_pairs={{0,8},{8,16},{16,24},{24,32},{32,40},{40,48},{48,56},{56,64},{64,7... | collective-permute-start | bytes 1181960 | tf_op jit(solution)/shard_map/while/body/eval_jaxpr/ppermute | solution.py:18
  344.7 12.5 %collective-permute-start = (bf16[513,384]{1,0:T(8,128)(2,1)}, bf16[513,384]{1,0:T(8,128)(2,1)}, u32[]{:S(2)}, u32[]{:S(2)}) collective-permute-start(bf16[513,384]{1,0:T(8,128)(2,1)} %copy.78), channel_id=1, source_target_pairs={{0,8},{8,16},{16,24},{24,32},{32,40},{40,48},{48,56},{56,64},{64,7... | collective-permute-start | bytes 1181960 | tf_op jit(solution)/shard_map/while/body/eval_jaxpr/ppermute | solution.py:18
  358.9 12.5 %collective-permute-start = (bf16[513,384]{1,0:T(8,128)(2,1)}, bf16[513,384]{1,0:T(8,128)(2,1)}, u32[]{:S(2)}, u32[]{:S(2)}) collective-permute-start(bf16[513,384]{1,0:T(8,128)(2,1)} %copy.78), channel_id=1, source_target_pairs={{0,8},{8,16},{16,24},{24,32},{32,40},{40,48},{48,56},{56,64},{64,7... | collective-permute-start | bytes 1181960 | tf_op jit(solution)/shard_map/while/body/eval_jaxpr/ppermute | solution.py:18
  373.2 13.1 %collective-permute-start = (bf16[513,384]{1,0:T(8,128)(2,1)}, bf16[513,384]{1,0:T(8,128)(2,1)}, u32[]{:S(2)}, u32[]{:S(2)}) collective-permute-start(bf16[513,384]{1,0:T(8,128)(2,1)} %copy.78), channel_id=1, source_target_pairs={{0,8},{8,16},{16,24},{24,32},{32,40},{40,48},{48,56},{56,64},{64,7... | collective-permute-start | bytes 1181960 | tf_op jit(solution)/shard_map/while/body/eval_jaxpr/ppermute | solution.py:18
  388.1 13.8 %collective-permute-start = (bf16[513,384]{1,0:T(8,128)(2,1)}, bf16[513,384]{1,0:T(8,128)(2,1)}, u32[]{:S(2)}, u32[]{:S(2)}) collective-permute-start(bf16[513,384]{1,0:T(8,128)(2,1)} %copy.78), channel_id=1, source_target_pairs={{0,8},{8,16},{16,24},{24,32},{32,40},{40,48},{48,56},{56,64},{64,7... | collective-permute-start | bytes 1181960 | tf_op jit(solution)/shard_map/while/body/eval_jaxpr/ppermute | solution.py:18
  403.6 13.8 %collective-permute-start = (bf16[513,384]{1,0:T(8,128)(2,1)}, bf16[513,384]{1,0:T(8,128)(2,1)}, u32[]{:S(2)}, u32[]{:S(2)}) collective-permute-start(bf16[513,384]{1,0:T(8,128)(2,1)} %copy.78), channel_id=1, source_target_pairs={{0,8},{8,16},{16,24},{24,32},{32,40},{40,48},{48,56},{56,64},{64,7... | collective-permute-start | bytes 1181960 | tf_op jit(solution)/shard_map/while/body/eval_jaxpr/ppermute | solution.py:18
  419.3 13.7 %collective-permute-start = (bf16[513,384]{1,0:T(8,128)(2,1)}, bf16[513,384]{1,0:T(8,128)(2,1)}, u32[]{:S(2)}, u32[]{:S(2)}) collective-permute-start(bf16[513,384]{1,0:T(8,128)(2,1)} %copy.78), channel_id=1, source_target_pairs={{0,8},{8,16},{16,24},{24,32},{32,40},{40,48},{48,56},{56,64},{64,7... | collective-permute-start | bytes 1181960 | tf_op jit(solution)/shard_map/while/body/eval_jaxpr/ppermute | solution.py:18
  434.7 13.6 %collective-permute-start = (bf16[513,384]{1,0:T(8,128)(2,1)}, bf16[513,384]{1,0:T(8,128)(2,1)}, u32[]{:S(2)}, u32[]{:S(2)}) collective-permute-start(bf16[513,384]{1,0:T(8,128)(2,1)} %copy.78), channel_id=1, source_target_pairs={{0,8},{8,16},{16,24},{24,32},{32,40},{40,48},{48,56},{56,64},{64,7... | collective-permute-start | bytes 1181960 | tf_op jit(solution)/shard_map/while/body/eval_jaxpr/ppermute | solution.py:18
  450.2 13.6 %collective-permute-start = (bf16[513,384]{1,0:T(8,128)(2,1)}, bf16[513,384]{1,0:T(8,128)(2,1)}, u32[]{:S(2)}, u32[]{:S(2)}) collective-permute-start(bf16[513,384]{1,0:T(8,128)(2,1)} %copy.78), channel_id=1, source_target_pairs={{0,8},{8,16},{16,24},{24,32},{32,40},{40,48},{48,56},{56,64},{64,7... | collective-permute-start | bytes 1181960 | tf_op jit(solution)/shard_map/while/body/eval_jaxpr/ppermute | solution.py:18
  465.5 13.6 %collective-permute-start = (bf16[513,384]{1,0:T(8,128)(2,1)}, bf16[513,384]{1,0:T(8,128)(2,1)}, u32[]{:S(2)}, u32[]{:S(2)}) collective-permute-start(bf16[513,384]{1,0:T(8,128)(2,1)} %copy.78), channel_id=1, source_target_pairs={{0,8},{8,16},{16,24},{24,32},{32,40},{40,48},{48,56},{56,64},{64,7... | collective-permute-start | bytes 1181960 | tf_op jit(solution)/shard_map/while/body/eval_jaxpr/ppermute | solution.py:18
  480.8 13.5 %collective-permute-start = (bf16[513,384]{1,0:T(8,128)(2,1)}, bf16[513,384]{1,0:T(8,128)(2,1)}, u32[]{:S(2)}, u32[]{:S(2)}) collective-permute-start(bf16[513,384]{1,0:T(8,128)(2,1)} %copy.78), channel_id=1, source_target_pairs={{0,8},{8,16},{16,24},{24,32},{32,40},{40,48},{48,56},{56,64},{64,7... | collective-permute-start | bytes 1181960 | tf_op jit(solution)/shard_map/while/body/eval_jaxpr/ppermute | solution.py:18
  (24 other events, 978.3 us)
Sparse Core Ops, SparseCore 0:
  503.5 148.0 reduce-scatter.3
where the time goes:
time: 684 us; the launch traced here: 679 us
  local copies, waits for them, and re-layouts  171 us (25%)
  starting transfers between devices  162 us (24%)
  waiting for transfers between devices  147 us (21%)
  matrix products  118 us (17%)
  blocking collectives  46.7 us (7%)
  other arithmetic  18.6 us (3%)
  between operations  14.4 us (2%)
    ppermute x32, starting transfers between devices, passed_along(): return lax.ppermute(block, axis, route)  162 us
    unnamed x2, waiting for transfers between devices  147 us
    dot_general x33, matrix products, attend(): jnp.einsum('hqk,khd->hqd', unnormed.astype(jnp.bfloat16), val_heads, pref...  69.6 us
    slice x64, local copies, waits for them, and re-layouts, attend(): val_heads = block[1].reshape(key_count, head_count, HEAD_DIM)  59.8 us
    another operation x31, local copies, waits for them, and re-layouts  55 us
    dot_general x33, matrix products, attend(): jnp.einsum('qhd,khd->hqk', query_heads, key_heads, preferred_element_type...  45.9 us
    pmin x1, blocking collectives, per_device(): first_tok = lax.pmin(local_first, 'seq')  28.3 us
    slice x32, local copies, waits for them, and re-layouts, attend(): key_heads = block[0].reshape(key_count, head_count, HEAD_DIM)  25.6 us
  transfers between devices with their start and end apart: 33, of which 2 were waited for; matrix products, arithmetic and copies ran while one was open for 35% of the time, Pallas kernels for 0%

commit v1 on v0

--- a/solution.py
+++ b/solution.py
@@ -133,7 +133,7 @@
     ).astype(jnp.float32)
     hidden_out = (hidden.astype(jnp.float32) + own_sum).astype(jnp.bfloat16)
     stream_wide = hidden_out.astype(jnp.float32)
-    square_total = lax.psum(jnp.sum(stream_wide * stream_wide, axis=1), "tp")
+    square_total = jnp.sum(lax.all_gather(jnp.sum(stream_wide * stream_wide, axis=1), "tp"), axis=0)
     normed = (
         stream_wide
         * lax.rsqrt(square_total / D + norm_epsilon)[:, None]

time: 684 us -> 684 us (level)
    psum x1 -> x0, blocking collectives: 18.4 us -> none  [per_device(): square_total = lax.psum(jnp.sum(stream_wide * stream_wide, axis=1), 'tp')]
    all_gather x0 -> x1, blocking collectives: none -> 17.5 us  [per_device(): lax.all_gather(jnp.sum(stream_wide * stream_wide, axis=1), 'tp')]
where the time goes in v1:
time: 684 us; the launch traced here: 678 us
  local copies, waits for them, and re-layouts  171 us (25%)
  starting transfers between devices  162 us (24%)
  waiting for transfers between devices  147 us (21%)
  matrix products  118 us (17%)
  blocking collectives  45.8 us (7%)
  other arithmetic  18.6 us (3%)
  between operations  14.4 us (2%)
    ppermute x32, starting transfers between devices, passed_along(): return lax.ppermute(block, axis, route)  162 us
    unnamed x2, waiting for transfers between devices  147 us
    dot_general x33, matrix products, attend(): jnp.einsum('hqk,khd->hqd', unnormed.astype(jnp.bfloat16), val_heads, pref...  69.6 us
    slice x64, local copies, waits for them, and re-layouts, attend(): val_heads = block[1].reshape(key_count, head_count, HEAD_DIM)  59.8 us
    another operation x31, local copies, waits for them, and re-layouts  55 us
    dot_general x33, matrix products, attend(): jnp.einsum('qhd,khd->hqk', query_heads, key_heads, preferred_element_type...  45.9 us
    pmin x1, blocking collectives, per_device(): first_tok = lax.pmin(local_first, 'seq')  28.3 us
    slice x32, local copies, waits for them, and re-layouts, attend(): key_heads = block[0].reshape(key_count, head_count, HEAD_DIM)  25.6 us
  transfers between devices with their start and end apart: 33, of which 2 were waited for; matrix products, arithmetic and copies ran while one was open for 35% of the time, Pallas kernels for 0%

profile of v1, /device:TPU:8, one launch (start us, length us, event | category | flops | bytes accessed | tf_op | source)
XLA Modules:
  0.0 678.0 jit_solution(3858717579963422848)
XLA Ops:
  8.2 28.3 %pmin.7 = s32[32]{0:T(128)S(1)} all-reduce(s32[32]{0:T(128)S(1)} %select_reduce_fusion.1), channel_id=1, replica_groups=mesh['seq'=64,'tp'=8] {'seq'}, use_global_device_ids=true, to_apply=%region_1.2 | all-reduce | flops 32 | bytes 256 | tf_op jit(solution)/shard_map/pmin | solution.py:85
  50.9 443.5 %while.16 = (s32[]{:T(128)}, f32[4,256]{1,0:T(4,128)S(1)}, f32[4,256]{1,0:T(4,128)S(1)}, f32[4,256,96]{1,2,0:T(8,128)}, bf16[513,384]{1,0:T(8,128)(2,1)}, /*inde...) while((s32[]{:T(128)}, f32[4,256]{1,0:T(4,128)S(1)}, f32[4,256]{1,0:T(4,128)S(1)}, ...), condition=%wide.region_8.9_spmd, body=%wide.region_5.8_spmd.sunk | while | flops 103286784 | bytes 8788605 | solution.py:121
  111.1 3.4 collective-permute-start
  160.9 3.3 collective-permute-start
  210.7 3.5 collective-permute-start
  223.4 9.2 %collective-permute-start = (bf16[513,384]{1,0:T(8,128)(2,1)}, bf16[513,384]{1,0:T(8,128)(2,1)}, u32[]{:S(2)}, u32[]{:S(2)}) collective-permute-start(bf16[513,384]{1,0:T(8,128)(2,1)} %copy.78), channel_id=1, source_target_pairs={{0,8},{8,16},{16,24},{24,32},{32,40},{40,48},{48,56},{56,64},{64,7... | collective-permute-start | bytes 1181960 | tf_op jit(solution)/shard_map/while/body/eval_jaxpr/ppermute | solution.py:18
  241.7 8.9 %collective-permute-start = (bf16[513,384]{1,0:T(8,128)(2,1)}, bf16[513,384]{1,0:T(8,128)(2,1)}, u32[]{:S(2)}, u32[]{:S(2)}) collective-permute-start(bf16[513,384]{1,0:T(8,128)(2,1)} %copy.78), channel_id=1, source_target_pairs={{0,8},{8,16},{16,24},{24,32},{32,40},{40,48},{48,56},{56,64},{64,7... | collective-permute-start | bytes 1181960 | tf_op jit(solution)/shard_map/while/body/eval_jaxpr/ppermute | solution.py:18
  259.8 9.4 %collective-permute-start = (bf16[513,384]{1,0:T(8,128)(2,1)}, bf16[513,384]{1,0:T(8,128)(2,1)}, u32[]{:S(2)}, u32[]{:S(2)}) collective-permute-start(bf16[513,384]{1,0:T(8,128)(2,1)} %copy.78), channel_id=1, source_target_pairs={{0,8},{8,16},{16,24},{24,32},{32,40},{40,48},{48,56},{56,64},{64,7... | collective-permute-start | bytes 1181960 | tf_op jit(solution)/shard_map/while/body/eval_jaxpr/ppermute | solution.py:18
  278.3 9.2 %collective-permute-start = (bf16[513,384]{1,0:T(8,128)(2,1)}, bf16[513,384]{1,0:T(8,128)(2,1)}, u32[]{:S(2)}, u32[]{:S(2)}) collective-permute-start(bf16[513,384]{1,0:T(8,128)(2,1)} %copy.78), channel_id=1, source_target_pairs={{0,8},{8,16},{16,24},{24,32},{32,40},{40,48},{48,56},{56,64},{64,7... | collective-permute-start | bytes 1181960 | tf_op jit(solution)/shard_map/while/body/eval_jaxpr/ppermute | solution.py:18
  296.6 8.4 %collective-permute-start = (bf16[513,384]{1,0:T(8,128)(2,1)}, bf16[513,384]{1,0:T(8,128)(2,1)}, u32[]{:S(2)}, u32[]{:S(2)}) collective-permute-start(bf16[513,384]{1,0:T(8,128)(2,1)} %copy.78), channel_id=1, source_target_pairs={{0,8},{8,16},{16,24},{24,32},{32,40},{40,48},{48,56},{56,64},{64,7... | collective-permute-start | bytes 1181960 | tf_op jit(solution)/shard_map/while/body/eval_jaxpr/ppermute | solution.py:18
  314.2 7.1 %collective-permute-start = (bf16[513,384]{1,0:T(8,128)(2,1)}, bf16[513,384]{1,0:T(8,128)(2,1)}, u32[]{:S(2)}, u32[]{:S(2)}) collective-permute-start(bf16[513,384]{1,0:T(8,128)(2,1)} %copy.78), channel_id=1, source_target_pairs={{0,8},{8,16},{16,24},{24,32},{32,40},{40,48},{48,56},{56,64},{64,7... | collective-permute-start | bytes 1181960 | tf_op jit(solution)/shard_map/while/body/eval_jaxpr/ppermute | solution.py:18
  330.4 5.1 collective-permute-start
  344.7 5.1 collective-permute-start
  358.9 5.1 collective-permute-start
  373.2 5.7 collective-permute-start
  388.1 6.5 collective-permute-start
  403.6 6.5 collective-permute-start
  419.3 6.4 collective-permute-start
  434.7 6.3 collective-permute-start
  450.2 6.2 collective-permute-start
  465.5 6.2 collective-permute-start
  480.8 6.2 collective-permute-start
  504.7 146.8 %reduce-scatter.4.cloned.1.call-done = bf16[384,256]{1,0:T(8,128)(2,1)} async-done(((bf16[3072,256]{1,0:T(8,128)(2,1)}), bf16[384,256]{1,0:T(8,128)(2,1)}) %reduce-scatter.4.cloned.1.call-update) | async-done | bytes 196624
  652.8 17.5 %all-gather.1 = f32[8,1,256]{2,1,0:T(1,128)S(1)} all-gather(f32[1,1,256]{2,1,0:T(1,128)S(1)} %bitcast.53), channel_id=2, replica_groups=mesh['seq'=64,'tp'=8] {'tp'}, dimensions={0}, use_global_device_ids=true | all-gather | bytes 9216 | tf_op jit(solution)/shard_map/all_gather | solution.py:136
  (498 shorter events, 342.0 us)
Async XLA Ops:
  7.2 644.4 %reduce-scatter.4.cloned.1.call-start = ((), (), s32[]{:S(2)}) async-start(), calls=%async_computation.1 | async-start | bytes 1769472
  111.1 10.7 %collective-permute-start = (bf16[513,384]{1,0:T(8,128)(2,1)}, bf16[513,384]{1,0:T(8,128)(2,1)}, u32[]{:S(2)}, u32[]{:S(2)}) collective-permute-start(bf16[513,384]{1,0:T(8,128)(2,1)} %copy.78), channel_id=1, source_target_pairs={{0,8},{8,16},{16,24},{24,32},{32,40},{40,48},{48,56},{56,64},{64,7... | collective-permute-start | bytes 1181960 | tf_op jit(solution)/shard_map/while/body/eval_jaxpr/ppermute | solution.py:18
  123.6 10.7 %collective-permute-start = (bf16[513,384]{1,0:T(8,128)(2,1)}, bf16[513,384]{1,0:T(8,128)(2,1)}, u32[]{:S(2)}, u32[]{:S(2)}) collective-permute-start(bf16[513,384]{1,0:T(8,128)(2,1)} %copy.78), channel_id=1, source_target_pairs={{0,8},{8,16},{16,24},{24,32},{32,40},{40,48},{48,56},{56,64},{64,7... | collective-permute-start | bytes 1181960 | tf_op jit(solution)/shard_map/while/body/eval_jaxpr/ppermute | solution.py:18
  160.9 10.7 %collective-permute-start = (bf16[513,384]{1,0:T(8,128)(2,1)}, bf16[513,384]{1,0:T(8,128)(2,1)}, u32[]{:S(2)}, u32[]{:S(2)}) collective-permute-start(bf16[513,384]{1,0:T(8,128)(2,1)} %copy.78), channel_id=1, source_target_pairs={{0,8},{8,16},{16,24},{24,32},{32,40},{40,48},{48,56},{56,64},{64,7... | collective-permute-start | bytes 1181960 | tf_op jit(solution)/shard_map/while/body/eval_jaxpr/ppermute | solution.py:18
  173.4 10.7 %collective-permute-start = (bf16[513,384]{1,0:T(8,128)(2,1)}, bf16[513,384]{1,0:T(8,128)(2,1)}, u32[]{:S(2)}, u32[]{:S(2)}) collective-permute-start(bf16[513,384]{1,0:T(8,128)(2,1)} %copy.78), channel_id=1, source_target_pairs={{0,8},{8,16},{16,24},{24,32},{32,40},{40,48},{48,56},{56,64},{64,7... | collective-permute-start | bytes 1181960 | tf_op jit(solution)/shard_map/while/body/eval_jaxpr/ppermute | solution.py:18
  198.3 10.7 %collective-permute-start = (bf16[513,384]{1,0:T(8,128)(2,1)}, bf16[513,384]{1,0:T(8,128)(2,1)}, u32[]{:S(2)}, u32[]{:S(2)}) collective-permute-start(bf16[513,384]{1,0:T(8,128)(2,1)} %copy.78), channel_id=1, source_target_pairs={{0,8},{8,16},{16,24},{24,32},{32,40},{40,48},{48,56},{56,64},{64,7... | collective-permute-start | bytes 1181960 | tf_op jit(solution)/shard_map/while/body/eval_jaxpr/ppermute | solution.py:18
  210.7 10.9 %collective-permute-start = (bf16[513,384]{1,0:T(8,128)(2,1)}, bf16[513,384]{1,0:T(8,128)(2,1)}, u32[]{:S(2)}, u32[]{:S(2)}) collective-permute-start(bf16[513,384]{1,0:T(8,128)(2,1)} %copy.78), channel_id=1, source_target_pairs={{0,8},{8,16},{16,24},{24,32},{32,40},{40,48},{48,56},{56,64},{64,7... | collective-permute-start | bytes 1181960 | tf_op jit(solution)/shard_map/while/body/eval_jaxpr/ppermute | solution.py:18
  223.4 16.5 %collective-permute-start = (bf16[513,384]{1,0:T(8,128)(2,1)}, bf16[513,384]{1,0:T(8,128)(2,1)}, u32[]{:S(2)}, u32[]{:S(2)}) collective-permute-start(bf16[513,384]{1,0:T(8,128)(2,1)} %copy.78), channel_id=1, source_target_pairs={{0,8},{8,16},{16,24},{24,32},{32,40},{40,48},{48,56},{56,64},{64,7... | collective-permute-start | bytes 1181960 | tf_op jit(solution)/shard_map/while/body/eval_jaxpr/ppermute | solution.py:18
  241.7 16.3 %collective-permute-start = (bf16[513,384]{1,0:T(8,128)(2,1)}, bf16[513,384]{1,0:T(8,128)(2,1)}, u32[]{:S(2)}, u32[]{:S(2)}) collective-permute-start(bf16[513,384]{1,0:T(8,128)(2,1)} %copy.78), channel_id=1, source_target_pairs={{0,8},{8,16},{16,24},{24,32},{32,40},{40,48},{48,56},{56,64},{64,7... | collective-permute-start | bytes 1181960 | tf_op jit(solution)/shard_map/while/body/eval_jaxpr/ppermute | solution.py:18
  259.8 16.8 %collective-permute-start = (bf16[513,384]{1,0:T(8,128)(2,1)}, bf16[513,384]{1,0:T(8,128)(2,1)}, u32[]{:S(2)}, u32[]{:S(2)}) collective-permute-start(bf16[513,384]{1,0:T(8,128)(2,1)} %copy.78), channel_id=1, source_target_pairs={{0,8},{8,16},{16,24},{24,32},{32,40},{40,48},{48,56},{56,64},{64,7... | collective-permute-start | bytes 1181960 | tf_op jit(solution)/shard_map/while/body/eval_jaxpr/ppermute | solution.py:18
  278.3 16.6 %collective-permute-start = (bf16[513,384]{1,0:T(8,128)(2,1)}, bf16[513,384]{1,0:T(8,128)(2,1)}, u32[]{:S(2)}, u32[]{:S(2)}) collective-permute-start(bf16[513,384]{1,0:T(8,128)(2,1)} %copy.78), channel_id=1, source_target_pairs={{0,8},{8,16},{16,24},{24,32},{32,40},{40,48},{48,56},{56,64},{64,7... | collective-permute-start | bytes 1181960 | tf_op jit(solution)/shard_map/while/body/eval_jaxpr/ppermute | solution.py:18
  296.6 15.8 %collective-permute-start = (bf16[513,384]{1,0:T(8,128)(2,1)}, bf16[513,384]{1,0:T(8,128)(2,1)}, u32[]{:S(2)}, u32[]{:S(2)}) collective-permute-start(bf16[513,384]{1,0:T(8,128)(2,1)} %copy.78), channel_id=1, source_target_pairs={{0,8},{8,16},{16,24},{24,32},{32,40},{40,48},{48,56},{56,64},{64,7... | collective-permute-start | bytes 1181960 | tf_op jit(solution)/shard_map/while/body/eval_jaxpr/ppermute | solution.py:18
  314.2 14.5 %collective-permute-start = (bf16[513,384]{1,0:T(8,128)(2,1)}, bf16[513,384]{1,0:T(8,128)(2,1)}, u32[]{:S(2)}, u32[]{:S(2)}) collective-permute-start(bf16[513,384]{1,0:T(8,128)(2,1)} %copy.78), channel_id=1, source_target_pairs={{0,8},{8,16},{16,24},{24,32},{32,40},{40,48},{48,56},{56,64},{64,7... | collective-permute-start | bytes 1181960 | tf_op jit(solution)/shard_map/while/body/eval_jaxpr/ppermute | solution.py:18
  330.4 12.5 %collective-permute-start = (bf16[513,384]{1,0:T(8,128)(2,1)}, bf16[513,384]{1,0:T(8,128)(2,1)}, u32[]{:S(2)}, u32[]{:S(2)}) collective-permute-start(bf16[513,384]{1,0:T(8,128)(2,1)} %copy.78), channel_id=1, source_target_pairs={{0,8},{8,16},{16,24},{24,32},{32,40},{40,48},{48,56},{56,64},{64,7... | collective-permute-start | bytes 1181960 | tf_op jit(solution)/shard_map/while/body/eval_jaxpr/ppermute | solution.py:18
  344.7 12.5 %collective-permute-start = (bf16[513,384]{1,0:T(8,128)(2,1)}, bf16[513,384]{1,0:T(8,128)(2,1)}, u32[]{:S(2)}, u32[]{:S(2)}) collective-permute-start(bf16[513,384]{1,0:T(8,128)(2,1)} %copy.78), channel_id=1, source_target_pairs={{0,8},{8,16},{16,24},{24,32},{32,40},{40,48},{48,56},{56,64},{64,7... | collective-permute-start | bytes 1181960 | tf_op jit(solution)/shard_map/while/body/eval_jaxpr/ppermute | solution.py:18
  358.9 12.5 %collective-permute-start = (bf16[513,384]{1,0:T(8,128)(2,1)}, bf16[513,384]{1,0:T(8,128)(2,1)}, u32[]{:S(2)}, u32[]{:S(2)}) collective-permute-start(bf16[513,384]{1,0:T(8,128)(2,1)} %copy.78), channel_id=1, source_target_pairs={{0,8},{8,16},{16,24},{24,32},{32,40},{40,48},{48,56},{56,64},{64,7... | collective-permute-start | bytes 1181960 | tf_op jit(solution)/shard_map/while/body/eval_jaxpr/ppermute | solution.py:18
  373.2 13.1 %collective-permute-start = (bf16[513,384]{1,0:T(8,128)(2,1)}, bf16[513,384]{1,0:T(8,128)(2,1)}, u32[]{:S(2)}, u32[]{:S(2)}) collective-permute-start(bf16[513,384]{1,0:T(8,128)(2,1)} %copy.78), channel_id=1, source_target_pairs={{0,8},{8,16},{16,24},{24,32},{32,40},{40,48},{48,56},{56,64},{64,7... | collective-permute-start | bytes 1181960 | tf_op jit(solution)/shard_map/while/body/eval_jaxpr/ppermute | solution.py:18
  388.1 13.8 %collective-permute-start = (bf16[513,384]{1,0:T(8,128)(2,1)}, bf16[513,384]{1,0:T(8,128)(2,1)}, u32[]{:S(2)}, u32[]{:S(2)}) collective-permute-start(bf16[513,384]{1,0:T(8,128)(2,1)} %copy.78), channel_id=1, source_target_pairs={{0,8},{8,16},{16,24},{24,32},{32,40},{40,48},{48,56},{56,64},{64,7... | collective-permute-start | bytes 1181960 | tf_op jit(solution)/shard_map/while/body/eval_jaxpr/ppermute | solution.py:18
  403.6 13.8 %collective-permute-start = (bf16[513,384]{1,0:T(8,128)(2,1)}, bf16[513,384]{1,0:T(8,128)(2,1)}, u32[]{:S(2)}, u32[]{:S(2)}) collective-permute-start(bf16[513,384]{1,0:T(8,128)(2,1)} %copy.78), channel_id=1, source_target_pairs={{0,8},{8,16},{16,24},{24,32},{32,40},{40,48},{48,56},{56,64},{64,7... | collective-permute-start | bytes 1181960 | tf_op jit(solution)/shard_map/while/body/eval_jaxpr/ppermute | solution.py:18
  419.3 13.7 %collective-permute-start = (bf16[513,384]{1,0:T(8,128)(2,1)}, bf16[513,384]{1,0:T(8,128)(2,1)}, u32[]{:S(2)}, u32[]{:S(2)}) collective-permute-start(bf16[513,384]{1,0:T(8,128)(2,1)} %copy.78), channel_id=1, source_target_pairs={{0,8},{8,16},{16,24},{24,32},{32,40},{40,48},{48,56},{56,64},{64,7... | collective-permute-start | bytes 1181960 | tf_op jit(solution)/shard_map/while/body/eval_jaxpr/ppermute | solution.py:18
  434.7 13.6 %collective-permute-start = (bf16[513,384]{1,0:T(8,128)(2,1)}, bf16[513,384]{1,0:T(8,128)(2,1)}, u32[]{:S(2)}, u32[]{:S(2)}) collective-permute-start(bf16[513,384]{1,0:T(8,128)(2,1)} %copy.78), channel_id=1, source_target_pairs={{0,8},{8,16},{16,24},{24,32},{32,40},{40,48},{48,56},{56,64},{64,7... | collective-permute-start | bytes 1181960 | tf_op jit(solution)/shard_map/while/body/eval_jaxpr/ppermute | solution.py:18
  450.2 13.6 %collective-permute-start = (bf16[513,384]{1,0:T(8,128)(2,1)}, bf16[513,384]{1,0:T(8,128)(2,1)}, u32[]{:S(2)}, u32[]{:S(2)}) collective-permute-start(bf16[513,384]{1,0:T(8,128)(2,1)} %copy.78), channel_id=1, source_target_pairs={{0,8},{8,16},{16,24},{24,32},{32,40},{40,48},{48,56},{56,64},{64,7... | collective-permute-start | bytes 1181960 | tf_op jit(solution)/shard_map/while/body/eval_jaxpr/ppermute | solution.py:18
  465.5 13.6 %collective-permute-start = (bf16[513,384]{1,0:T(8,128)(2,1)}, bf16[513,384]{1,0:T(8,128)(2,1)}, u32[]{:S(2)}, u32[]{:S(2)}) collective-permute-start(bf16[513,384]{1,0:T(8,128)(2,1)} %copy.78), channel_id=1, source_target_pairs={{0,8},{8,16},{16,24},{24,32},{32,40},{40,48},{48,56},{56,64},{64,7... | collective-permute-start | bytes 1181960 | tf_op jit(solution)/shard_map/while/body/eval_jaxpr/ppermute | solution.py:18
  480.8 13.5 %collective-permute-start = (bf16[513,384]{1,0:T(8,128)(2,1)}, bf16[513,384]{1,0:T(8,128)(2,1)}, u32[]{:S(2)}, u32[]{:S(2)}) collective-permute-start(bf16[513,384]{1,0:T(8,128)(2,1)} %copy.78), channel_id=1, source_target_pairs={{0,8},{8,16},{16,24},{24,32},{32,40},{40,48},{48,56},{56,64},{64,7... | collective-permute-start | bytes 1181960 | tf_op jit(solution)/shard_map/while/body/eval_jaxpr/ppermute | solution.py:18
  (24 other events, 976.6 us)
Sparse Core Ops, SparseCore 0:
  503.5 148.0 reduce-scatter.3
